TPU v7x, 256 devices: a whole 4x4x8 slice. The times are simulated.
256 devices in a mesh: gx: 32 (over x, y, core), gy: 8 (over z).
Axes of the slice: x: 4, y: 4, z: 8, core: 2. Of those that a mesh axis runs over, the one named last changes fastest.
Arguments:
- orbitals: float32 [64, 128, 64, 128], P(None, 'gx', 'gy'), may hold values from -60 to 60, as said below
- potential: float32 [128, 64, 128], P('gx', 'gy'), may hold values from 0.2 to 2
Outputs:
- basis: float32 [64, 128, 64, 128], P(None, 'gx', 'gy')
- factor: float32 [64, 64], replicated
Inputs may be any that keep to these rules, and one draw needn't show every extreme that they name: `orbitals`: Real-valued entries.
All inputs are finite; a program needn't handle non-finite values.
Results may differ from a plain program's by a relative error of at most 0.00011.
Values sent between devices are 32-bit elements; how exact they have to be, the bound alone decides.
No kernel may reach another device: no remote copies, remote signals or barrier semaphores. Data moves between devices by JAX's collectives and lax.ppermute only.
A program may use at most 64 MiB of HBM per device.

v0:
```python
import jax
import jax.numpy as jnp
from jax import lax
from jax.sharding import PartitionSpec as P


def extended(cells, sides, width):
    for axis, dim in sides:
        count = lax.axis_size(axis)
        head = lax.slice_in_dim(cells, 0, width, axis=dim)
        tail = lax.slice_in_dim(cells, cells.shape[dim] - width, cells.shape[dim], axis=dim)
        cells = jnp.concatenate(
            [
                lax.ppermute(tail, axis, [(i, (i + 1) % count) for i in range(count)]),
                cells,
                lax.ppermute(head, axis, [((i + 1) % count, i) for i in range(count)]),
            ],
            axis=dim,
        )
    return cells


def apply_ham(padded, pot):
    core = padded[:, 2:-2, 2:-2]
    total = -7.5 * core
    total = total + 4.0 / 3.0 * (padded[:, 3:-1, 2:-2] + padded[:, 1:-3, 2:-2])
    total = total - 1.0 / 12.0 * (padded[:, 4:, 2:-2] + padded[:, :-4, 2:-2])
    total = total + 4.0 / 3.0 * (padded[:, 2:-2, 3:-1] + padded[:, 2:-2, 1:-3])
    total = total - 1.0 / 12.0 * (padded[:, 2:-2, 4:] + padded[:, 2:-2, :-4])
    total = total + 4.0 / 3.0 * (jnp.roll(core, 1, 3) + jnp.roll(core, -1, 3))
    total = total - 1.0 / 12.0 * (jnp.roll(core, 2, 3) + jnp.roll(core, -2, 3))
    return -0.5 * total + pot[None] * core


def with_faces(field):
    return extended(field, (("gx", 1), ("gy", 2)), 2)


def upper_factor(gram):
    order = gram.shape[0]
    index = jnp.arange(order)

    def column_step(col, lower):
        row_now = lax.dynamic_slice_in_dim(lower, col, 1, 0)[0]
        target = lax.dynamic_slice_in_dim(gram, col, 1, 1)[:, 0]
        column = target - jnp.dot(
            lower, row_now, precision=lax.Precision.HIGHEST, preferred_element_type=jnp.float32
        )
        pivot = jnp.sqrt(jnp.sum(jnp.where(index == col, column, 0.0)))
        values = jnp.where(index == col, pivot, column / pivot)
        values = jnp.where(index >= col, values, 0.0)
        return jnp.where(index[None, :] == col, values[:, None], lower)

    lower = lax.fori_loop(0, order, column_step, jnp.zeros_like(gram))
    return lower.T


def upper_inverse(upper):
    order = upper.shape[0]
    index = jnp.arange(order)

    def row_step(step, inverse):
        row = order - 1 - step
        upper_row = lax.dynamic_slice_in_dim(upper, row, 1, 0)[0]
        pivot = jnp.sum(jnp.where(index == row, upper_row, 0.0))
        rest = jnp.dot(
            upper_row, inverse, precision=lax.Precision.HIGHEST, preferred_element_type=jnp.float32
        )
        unit = jnp.where(index == row, 1.0, 0.0).astype(jnp.float32)
        new_row = (unit - rest) / pivot
        return jnp.where(index[:, None] == row, new_row[None, :], inverse)

    return lax.fori_loop(0, order, row_step, jnp.zeros_like(upper))


def shards(orbitals, potential):
    first = (apply_ham(with_faces(orbitals), potential) - 5.5 * orbitals) / 4.5
    applied = apply_ham(with_faces(first), potential)
    filtered = 2.0 * (applied - 5.5 * first) / 4.5 - orbitals
    width = filtered.shape[0]
    flat = filtered.reshape(width, -1)
    cells = flat.shape[1] * lax.axis_size("gx") * lax.axis_size("gy")
    local_gram = (
        jnp.dot(flat, flat.T, precision=lax.Precision.HIGHEST, preferred_element_type=jnp.float32)
        / cells
    )
    factor = upper_factor(lax.psum(local_gram, ("gx", "gy")))
    inverse = upper_inverse(factor)
    solved = jnp.dot(
        inverse.T, flat, precision=lax.Precision.HIGHEST, preferred_element_type=jnp.float32
    )
    basis = (solved * jnp.sqrt(jnp.float32(cells))).reshape(filtered.shape)
    return (basis, factor)


def solution(mesh):
    return jax.shard_map(
        shards,
        mesh=mesh,
        in_specs=(P(None, "gx", "gy", None), P("gx", "gy", None)),
        out_specs=(P(None, "gx", "gy", None), P()),
        check_vma=False,
    )
```

profile of v0, /device:TPU:1, one launch (start us, length us, event | category | flops | bytes accessed | tf_op | source)
XLA Modules:
  0.0 353.4 jit_solution(158170441676691293)
XLA Ops:
  0.6 2.4 fusion.60
  3.0 3.2 collective-permute-start
  8.3 4.5 %collective-permute-done = f32[64,2,8,128]{3,2,1,0:T(8,128)S(1)} collective-permute-done((f32[64,2,8,128]{3,2,1,0:T(8,128)}, f32[64,2,8,128]{3,2,1,0:T(8,128)S(1)}, u32[]{:S(2)}, u32[]{:S(2)}) %collective-permute-start) | collective-permute-done | bytes 524320 | tf_op jit(solution)/shard_map/ppermute | solution.py:16
  13.7 5.7 %collective-permute-start.2 = (f32[64,8,2,128]{3,1,2,0:T(8,128)S(1)}, f32[64,8,2,128]{3,1,2,0:T(8,128)S(1)}, u32[]{:S(2)}, u32[]{:S(2)}) collective-permute-start(f32[64,8,2,128]{3,1,2,0:T(8,128)S(1)} %get-tuple-element.266), channel_id=1, source_target_pairs={{1,0},{2,1},{3,2},{4,3},{5,4},{6,5},{7,6},{0,7},{9,8},{10,9},{11,1... | collective-permute-start | bytes 1572872 | tf_op jit(solution)/shard_map/ppermute | solution.py:16
  20.6 4.8 %collective-permute-done.2 = f32[64,8,2,128]{3,1,2,0:T(8,128)S(1)} collective-permute-done((f32[64,8,2,128]{3,1,2,0:T(8,128)S(1)}, f32[64,8,2,128]{3,1,2,0:T(8,128)S(1)}, u32[]{:S(2)}, u32[]{:S(2)}) %collective-permute-start.2) | collective-permute-done | bytes 524320 | tf_op jit(solution)/shard_map/ppermute | solution.py:16
  25.4 3.1 collective-permute-done.3
  28.6 7.3 %broadcast_multiply_fusion = (f32[64,4,8,128]{3,1,2,0:T(4,128)S(1)}, f32[64,4,8,128]{3,1,2,0:T(4,128)S(1)}) fusion(f32[64,4,8,128]{3,1,2,0:T(4,128)S(1)} %copy.55, f32[4,8,128]{2,0,1:T(4,128)S(1)} %copy.71, f32[64,4,8,2]{3,1,2,0:T(4,128)S(1)} %get-tuple-element.285, f32[64,4,8,126]{3,1,2,0:T(4,128)S(1)} %get-tuple-element.287, ...), kind=kLoop, calls=%fused_computation.105 | loop fusion | flops 11796480 | bytes 9453568 | tf_op jit(solution)/shard_map/div | solution.py:77
  36.4 9.8 %collective-permute-start.4 = (f32[64,2,8,128]{3,2,1,0:T(8,128)S(1)}, f32[64,2,8,128]{3,2,1,0:T(8,128)S(1)}, u32[]{:S(2)}, u32[]{:S(2)}) collective-permute-start(f32[64,2,8,128]{3,2,1,0:T(8,128)S(1)} %copy.74), channel_id=1, source_target_pairs={{8,0},{16,8},{24,16},{32,24},{40,32},{48,40},{56,48},{64,56},{72,6... | collective-permute-start | bytes 1572872 | tf_op jit(solution)/shard_map/ppermute | solution.py:16
  47.7 3.3 collective-permute-done.4
  51.3 1.3 collective-permute-done.5
  53.3 1.5 collective-permute-start.7
  56.0 5.3 %collective-permute-done.6 = f32[64,8,2,128]{3,1,2,0:T(8,128)S(1)} collective-permute-done((f32[64,8,2,128]{3,1,2,0:T(8,128)S(1)}, f32[64,8,2,128]{3,1,2,0:T(8,128)S(1)}, u32[]{:S(2)}, u32[]{:S(2)}) %collective-permute-start.6) | collective-permute-done | bytes 524320 | tf_op jit(solution)/shard_map/ppermute | solution.py:16
  61.3 1.3 collective-permute-done.7
  62.6 7.5 %multiply_subtract_fusion = f32[64,4,8,128]{3,1,2,0:T(4,128)S(1)} fusion(f32[64,4,8,128]{3,1,2,0:T(4,128)S(1)} %get-tuple-element.261, f32[64,4,8,2]{3,1,2,0:T(4,128)S(1)} %get-tuple-element.275, f32[64,4,8,126]{3,1,2,0:T(4,128)S(1)} %get-tuple-element.277, f32[64,4,8,126]{3,1,2,0:T(4,128)S(1)} %get-tuple-element.276, ...), kind=kLoop, calls=%fused_computation.97 | loop fusion | flops 12058624 | bytes 10502144 | tf_op jit(solution)/shard_map/sub | solution.py:79
  70.1 2.1 fusion.17
  72.2 81.9 %psum.7 = f32[64,64]{1,0:T(8,128)S(1)} all-reduce(f32[64,64]{1,0:T(8,128)S(1)} %fusion.17), channel_id=1, replica_groups=mesh['gx'=32,'gy'=8] {'gx','gy'}, use_global_device_ids=true, to_apply=%region_0.1 | all-reduce | flops 4096 | bytes 32768 | tf_op jit(solution)/shard_map/psum | solution.py:87
  154.2 101.3 %while.32 = (s32[]{:T(128)}, f32[64,64]{1,0:T(8,128)S(1)}, f32[64,64]{0,1:T(8,128)S(1)}, s32[]{:T(128)}, s32[]{:T(128)}) while((s32[]{:T(128)}, f32[64,64]{1,0:T(8,128)S(1)}, f32[64,64]{0,1:T(8,128)S(1)}, s32[]{:T(128)}, s32[]{:T(128)}) %tuple.94), condition=%wide.region_3.4_spmd.clone.clone, body=%wide.region_1.3_spmd.clone.clone.sunk | while | flops 62082 | bytes 102112 | solution.py:54
  255.6 95.1 %while.31 = (s32[]{:T(128)}, f32[64,64]{1,0:T(8,128)S(1)}, f32[64,64]{1,0:T(8,128)S(1)}, s32[]{:T(128)}, s32[]{:T(128)}, /*index=5*/s32[]{:T(128)}, s32[]{:T(128)}) while((s32[]{:T(128)}, f32[64,64]{1,0:T(8,128)S(1)}, f32[64,64]{1,0:T(8,128)S(1)}, s32[]{:T(128)}, s32[]{:T(128)}, /*index=5*/s32[]{:T(128)}, s32[]{:T(128)}) %tuple.100), condition=%wide.region_6.7_spmd.clone, body=%wide.region_4.6_spmd.clone.sunk | while | flops 61958 | bytes 67106 | solution.py:73
  256.2 0.8 fusion.75
  257.7 0.8 fusion.75
  259.1 0.8 fusion.75
  262.1 0.8 fusion.75
  263.6 0.8 fusion.75
  265.1 0.8 fusion.75
  266.6 0.8 fusion.75
  268.1 0.8 fusion.75
  271.0 0.8 fusion.75
  272.5 0.8 fusion.75
  274.0 0.8 fusion.75
  275.5 0.8 fusion.75
  277.0 0.8 fusion.75
  278.5 0.8 fusion.75
  279.9 0.8 fusion.75
  281.4 0.8 fusion.75
  282.9 0.8 fusion.75
  284.4 0.8 fusion.75
  285.9 0.8 fusion.75
  287.4 0.8 fusion.75
  290.3 0.8 fusion.75
  291.8 0.8 fusion.75
  293.3 0.8 fusion.75
  294.8 0.8 fusion.75
  296.3 0.8 fusion.75
  299.2 0.8 fusion.75
  300.7 0.8 fusion.75
  302.2 0.8 fusion.75
  303.7 0.8 fusion.75
  305.2 0.8 fusion.75
  306.7 0.8 fusion.75
  308.2 0.8 fusion.75
  309.6 0.8 fusion.75
  311.1 0.8 fusion.75
  312.6 0.8 fusion.75
  314.1 0.8 fusion.75
  315.6 0.8 fusion.75
  318.6 0.8 fusion.75
  320.0 0.8 fusion.75
  321.5 0.8 fusion.75
  323.0 0.8 fusion.75
  324.5 0.8 fusion.75
  327.5 0.8 fusion.75
  329.0 0.8 fusion.75
  350.6 1.6 fusion.16
  352.2 1.2 copy.89
  (569 shorter events, 124.5 us)
Async XLA Ops:
  0.6 5.6 %copy-start = (f32[64,4,8,128]{3,2,1,0:T(8,128)S(1)}, f32[64,4,8,128]{3,2,1,0:T(8,128)}, u32[]{:S(2)}) copy-start(f32[64,4,8,128]{3,2,1,0:T(8,128)} %param.6) | copy-start | bytes 3145732
  3.0 9.8 %collective-permute-start = (f32[64,2,8,128]{3,2,1,0:T(8,128)}, f32[64,2,8,128]{3,2,1,0:T(8,128)S(1)}, u32[]{:S(2)}, u32[]{:S(2)}) collective-permute-start(f32[64,2,8,128]{3,2,1,0:T(8,128)} %get-tuple-element.279), channel_id=1, source_target_pairs={{8,0},{16,8},{24,16},{32,24},{40,32},{48,40},{56,48},{64,56},{72,6... | collective-permute-start | bytes 1572872 | tf_op jit(solution)/shard_map/ppermute | solution.py:16
  6.2 0.7 copy-start.1
  6.2 6.8 %collective-permute-start.1 = (f32[64,2,8,128]{3,2,1,0:T(8,128)}, f32[64,2,8,128]{3,2,1,0:T(8,128)S(1)}, u32[]{:S(2)}, u32[]{:S(2)}) collective-permute-start(f32[64,2,8,128]{3,2,1,0:T(8,128)} %get-tuple-element.278), channel_id=1, source_target_pairs={{0,8},{8,16},{16,24},{24,32},{32,40},{40,48},{48,56},{56,64},{64,7... | collective-permute-start | bytes 1572872 | tf_op jit(solution)/shard_map/ppermute | solution.py:14
  13.7 11.8 %collective-permute-start.2 = (f32[64,8,2,128]{3,1,2,0:T(8,128)S(1)}, f32[64,8,2,128]{3,1,2,0:T(8,128)S(1)}, u32[]{:S(2)}, u32[]{:S(2)}) collective-permute-start(f32[64,8,2,128]{3,1,2,0:T(8,128)S(1)} %get-tuple-element.266), channel_id=1, source_target_pairs={{1,0},{2,1},{3,2},{4,3},{5,4},{6,5},{7,6},{0,7},{9,8},{10,9},{11,1... | collective-permute-start | bytes 1572872 | tf_op jit(solution)/shard_map/ppermute | solution.py:16
  19.3 9.2 %collective-permute-start.3 = (f32[64,8,2,128]{3,1,2,0:T(8,128)S(1)}, f32[64,8,2,128]{3,1,2,0:T(8,128)S(1)}, u32[]{:S(2)}, u32[]{:S(2)}) collective-permute-start(f32[64,8,2,128]{3,1,2,0:T(8,128)S(1)} %get-tuple-element.267), channel_id=1, source_target_pairs={{0,1},{1,2},{2,3},{3,4},{4,5},{5,6},{6,7},{7,0},{8,9},{9,10},{10,1... | collective-permute-start | bytes 1572872 | tf_op jit(solution)/shard_map/ppermute | solution.py:14
  36.4 14.6 %collective-permute-start.4 = (f32[64,2,8,128]{3,2,1,0:T(8,128)S(1)}, f32[64,2,8,128]{3,2,1,0:T(8,128)S(1)}, u32[]{:S(2)}, u32[]{:S(2)}) collective-permute-start(f32[64,2,8,128]{3,2,1,0:T(8,128)S(1)} %copy.74), channel_id=1, source_target_pairs={{8,0},{16,8},{24,16},{32,24},{40,32},{48,40},{56,48},{64,56},{72,6... | collective-permute-start | bytes 1572872 | tf_op jit(solution)/shard_map/ppermute | solution.py:16
  46.2 6.4 %collective-permute-start.5 = (f32[64,2,8,128]{3,2,1,0:T(8,128)S(1)}, f32[64,2,8,128]{3,2,1,0:T(8,128)S(1)}, u32[]{:S(2)}, u32[]{:S(2)}) collective-permute-start(f32[64,2,8,128]{3,2,1,0:T(8,128)S(1)} %copy.76), channel_id=1, source_target_pairs={{0,8},{8,16},{16,24},{24,32},{32,40},{40,48},{48,56},{56,64},{64,7... | collective-permute-start | bytes 1572872 | tf_op jit(solution)/shard_map/ppermute | solution.py:14
  53.2 8.1 %collective-permute-start.6 = (f32[64,8,2,128]{3,1,2,0:T(8,128)S(1)}, f32[64,8,2,128]{3,1,2,0:T(8,128)S(1)}, u32[]{:S(2)}, u32[]{:S(2)}) collective-permute-start(f32[64,8,2,128]{3,1,2,0:T(8,128)S(1)} %get-tuple-element.264), channel_id=1, source_target_pairs={{1,0},{2,1},{3,2},{4,3},{5,4},{6,5},{7,6},{0,7},{9,8},{10,9},{11,1... | collective-permute-start | bytes 1572872 | tf_op jit(solution)/shard_map/ppermute | solution.py:16
  53.3 9.3 %collective-permute-start.7 = (f32[64,8,2,128]{3,1,2,0:T(8,128)S(1)}, f32[64,8,2,128]{3,1,2,0:T(8,128)S(1)}, u32[]{:S(2)}, u32[]{:S(2)}) collective-permute-start(f32[64,8,2,128]{3,1,2,0:T(8,128)S(1)} %get-tuple-element.265), channel_id=1, source_target_pairs={{0,1},{1,2},{2,3},{3,4},{4,5},{5,6},{6,7},{7,0},{8,9},{9,10},{10,1... | collective-permute-start | bytes 1572872 | tf_op jit(solution)/shard_map/ppermute | solution.py:14
  350.6 1.6 copy-start.2
where the time goes:
time: 355 us; the launch traced here: 353 us
  matrix products  103 us (29%)
  blocking collectives  81.9 us (23%)
  other arithmetic  66.1 us (19%)
  loops' own time  46 us (13%)
  waiting for transfers between devices  23.6 us (7%)
  starting transfers between devices  20.4 us (6%)
  local copies, waits for them, and re-layouts  11.1 us (3%)
    psum x1, blocking collectives, shards(): factor = upper_factor(lax.psum(local_gram, ('gx', 'gy')))  81.9 us
    dot_general x64, matrix products, row_step(): jnp.dot(upper_row, inverse, precision=lax.Precision.HIGHEST, preferred_el...  50.1 us
    dot_general x64, matrix products, column_step(): jnp.dot(lower, row_now, precision=lax.Precision.HIGHEST, preferred_elemen...  49.5 us
    another operation x1, loops' own time, upper_factor(): lower = lax.fori_loop(0, order, column_step, jnp.zeros_like(gram))  45.6 us
    reduce_sum x64, other arithmetic, row_step(): pivot = jnp.sum(jnp.where(index == row, upper_row, 0.0))  39.3 us
    ppermute x4, starting transfers between devices, extended(): lax.ppermute(head, axis, [((i + 1) % count, i) for i in range(count)])  18.7 us
    ppermute x4, waiting for transfers between devices, extended(): lax.ppermute(head, axis, [((i + 1) % count, i) for i in range(count)])  17.9 us
    sub x1, other arithmetic, shards(): filtered = 2.0 * (applied - 5.5 * first) / 4.5 - orbitals  7.45 us
  transfers between devices with their start and end apart: 8, of which 7 were waited for; matrix products, arithmetic and copies ran while one was open for 2% of the time, Pallas kernels for 0%

commit v1 on v0

--- a/solution.py
+++ b/solution.py
@@ -84,7 +84,8 @@
         jnp.dot(flat, flat.T, precision=lax.Precision.HIGHEST, preferred_element_type=jnp.float32)
         / cells
     )
-    factor = upper_factor(lax.psum(local_gram, ("gx", "gy")))
+    _do_row = lambda inner_x, row_axis: jnp.sum(lax.all_gather(inner_x, row_axis), 0)
+    factor = upper_factor(_do_row(local_gram, ("gx", "gy")))
     inverse = upper_inverse(factor)
     solved = jnp.dot(
         inverse.T, flat, precision=lax.Precision.HIGHEST, preferred_element_type=jnp.float32

time: 355 us -> 411 us (1.16)
  waiting for transfers between devices: 23.6 us -> 145 us
  blocking collectives: 81.9 us -> 0 us
  between operations: 0.88 us -> 14.3 us
    all_gather x0 -> x1, waiting for transfers between devices: none -> 121 us  [shards(): lax.all_gather(inner_x, row_axis)]
    psum x1 -> x0, blocking collectives: 81.9 us -> none  [shards(): factor = upper_factor(lax.psum(local_gram, ('gx', 'gy')))]
  transfers between devices with their start and end apart: 8 -> 9, of which waited for: 7 -> 8; matrix products, arithmetic and copies ran while one was open for 2% -> 1% of each run, Pallas kernels for 0% -> 0%
where the time goes in v1:
time: 411 us; the launch traced here: 410 us
  waiting for transfers between devices  145 us (35%)
  matrix products  104 us (25%)
  other arithmetic  70.2 us (17%)
  loops' own time  46.1 us (11%)
  starting transfers between devices  20.6 us (5%)
  between operations  14.3 us (3%)
  local copies, waits for them, and re-layouts  9.71 us (2%)
    all_gather x1, waiting for transfers between devices, shards(): lax.all_gather(inner_x, row_axis)  121 us
    dot_general x64, matrix products, row_step(): jnp.dot(upper_row, inverse, precision=lax.Precision.HIGHEST, preferred_el...  50.1 us
    dot_general x64, matrix products, column_step(): jnp.dot(lower, row_now, precision=lax.Precision.HIGHEST, preferred_elemen...  49.5 us
    another operation x1, loops' own time, upper_factor(): lower = lax.fori_loop(0, order, column_step, jnp.zeros_like(gram))  45.6 us
    reduce_sum x64, other arithmetic, row_step(): pivot = jnp.sum(jnp.where(index == row, upper_row, 0.0))  39.3 us
    ppermute x4, starting transfers between devices, extended(): lax.ppermute(head, axis, [((i + 1) % count, i) for i in range(count)])  18.8 us
    ppermute x4, waiting for transfers between devices, extended(): lax.ppermute(head, axis, [((i + 1) % count, i) for i in range(count)])  18.2 us
  transfers between devices with their start and end apart: 9, of which 8 were waited for; matrix products, arithmetic and copies ran while one was open for 1% of the time, Pallas kernels for 0%

profile of v1, /device:TPU:1, one launch (start us, length us, event | category | flops | bytes accessed | tf_op | source)
XLA Modules:
  0.0 409.6 jit_solution(6983221593491255411)
XLA Ops:
  7.2 1.4 fusion.60
  8.6 3.3 collective-permute-start
  13.5 4.7 %collective-permute-done = f32[64,2,8,128]{3,2,1,0:T(8,128)S(1)} collective-permute-done((f32[64,2,8,128]{3,2,1,0:T(8,128)S(1)}, f32[64,2,8,128]{3,2,1,0:T(8,128)S(1)}, u32[]{:S(2)}, u32[]{:S(2)}) %collective-permute-start) | collective-permute-done | bytes 524320 | tf_op jit(solution)/shard_map/ppermute | solution.py:16
  19.1 5.7 %collective-permute-start.2 = (f32[64,8,2,128]{3,1,2,0:T(8,128)S(1)}, f32[64,8,2,128]{3,1,2,0:T(8,128)S(1)}, u32[]{:S(2)}, u32[]{:S(2)}) collective-permute-start(f32[64,8,2,128]{3,1,2,0:T(8,128)S(1)} %get-tuple-element.263), channel_id=1, source_target_pairs={{1,0},{2,1},{3,2},{4,3},{5,4},{6,5},{7,6},{0,7},{9,8},{10,9},{11,1... | collective-permute-start | bytes 1572872 | tf_op jit(solution)/shard_map/ppermute | solution.py:16
  26.1 4.8 %collective-permute-done.2 = f32[64,8,2,128]{3,1,2,0:T(8,128)S(1)} collective-permute-done((f32[64,8,2,128]{3,1,2,0:T(8,128)S(1)}, f32[64,8,2,128]{3,1,2,0:T(8,128)S(1)}, u32[]{:S(2)}, u32[]{:S(2)}) %collective-permute-start.2) | collective-permute-done | bytes 524320 | tf_op jit(solution)/shard_map/ppermute | solution.py:16
  30.9 3.1 collective-permute-done.3
  34.0 7.4 %broadcast_multiply_fusion = (f32[64,4,8,128]{3,1,2,0:T(4,128)S(1)}, f32[64,4,8,128]{3,1,2,0:T(4,128)S(1)}) fusion(f32[64,4,8,128]{3,1,2,0:T(4,128)S(1)} %copy.54, f32[4,8,128]{2,0,1:T(4,128)S(1)} %copy.70, f32[64,4,8,2]{3,1,2,0:T(4,128)S(1)} %get-tuple-element.282, f32[64,4,8,126]{3,1,2,0:T(4,128)S(1)} %get-tuple-element.284, ...), kind=kLoop, calls=%fused_computation.105 | loop fusion | flops 11796480 | bytes 9453568 | tf_op jit(solution)/shard_map/div | solution.py:77
  41.9 9.7 %collective-permute-start.4 = (f32[64,2,8,128]{3,2,1,0:T(8,128)S(1)}, f32[64,2,8,128]{3,2,1,0:T(8,128)S(1)}, u32[]{:S(2)}, u32[]{:S(2)}) collective-permute-start(f32[64,2,8,128]{3,2,1,0:T(8,128)S(1)} %copy.73), channel_id=1, source_target_pairs={{8,0},{16,8},{24,16},{32,24},{40,32},{48,40},{56,48},{64,56},{72,6... | collective-permute-start | bytes 1572872 | tf_op jit(solution)/shard_map/ppermute | solution.py:16
  53.2 3.4 collective-permute-done.4
  56.9 1.2 collective-permute-done.5
  58.8 1.5 collective-permute-start.7
  61.5 5.3 %collective-permute-done.6 = f32[64,8,2,128]{3,1,2,0:T(8,128)S(1)} collective-permute-done((f32[64,8,2,128]{3,1,2,0:T(8,128)S(1)}, f32[64,8,2,128]{3,1,2,0:T(8,128)S(1)}, u32[]{:S(2)}, u32[]{:S(2)}) %collective-permute-start.6) | collective-permute-done | bytes 524320 | tf_op jit(solution)/shard_map/ppermute | solution.py:16
  66.8 1.3 collective-permute-done.7
  68.1 7.5 %multiply_subtract_fusion = f32[64,4,8,128]{3,1,2,0:T(4,128)S(1)} fusion(f32[64,4,8,128]{3,1,2,0:T(4,128)S(1)} %get-tuple-element.258, f32[64,4,8,2]{3,1,2,0:T(4,128)S(1)} %get-tuple-element.272, f32[64,4,8,126]{3,1,2,0:T(4,128)S(1)} %get-tuple-element.274, f32[64,4,8,126]{3,1,2,0:T(4,128)S(1)} %get-tuple-element.273, ...), kind=kLoop, calls=%fused_computation.97 | loop fusion | flops 12058624 | bytes 10502144 | tf_op jit(solution)/shard_map/sub | solution.py:79
  75.5 2.7 fusion.17
  78.4 121.1 %all-gather.3.cloned.1.call-done = f32[16384,64]{1,0:T(8,128)} async-done(((f32[64,64]{1,0:T(8,128)}), f32[16384,64]{1,0:T(8,128)}) %all-gather.3.cloned.1.call-update) | async-done | bytes 4194320 | tf_op jit(solution)/shard_map/all_gather | solution.py:87
  199.5 4.0 reduce_sum.38
  203.5 101.3 %while.32 = (s32[]{:T(128)}, f32[64,64]{1,0:T(8,128)S(1)}, f32[64,64]{0,1:T(8,128)S(1)}, s32[]{:T(128)}, s32[]{:T(128)}) while((s32[]{:T(128)}, f32[64,64]{1,0:T(8,128)S(1)}, f32[64,64]{0,1:T(8,128)S(1)}, s32[]{:T(128)}, s32[]{:T(128)}) %tuple.93), condition=%wide.region_3.4_spmd.clone.clone, body=%wide.region_1.3_spmd.clone.clone.sunk | while | flops 62082 | bytes 102112 | solution.py:54
  304.9 95.1 %while.31 = (s32[]{:T(128)}, f32[64,64]{1,0:T(8,128)S(1)}, f32[64,64]{1,0:T(8,128)S(1)}, s32[]{:T(128)}, s32[]{:T(128)}, /*index=5*/s32[]{:T(128)}, s32[]{:T(128)}) while((s32[]{:T(128)}, f32[64,64]{1,0:T(8,128)S(1)}, f32[64,64]{1,0:T(8,128)S(1)}, s32[]{:T(128)}, s32[]{:T(128)}, /*index=5*/s32[]{:T(128)}, s32[]{:T(128)}) %tuple.101), condition=%wide.region_6.7_spmd.clone, body=%wide.region_4.6_spmd.clone.sunk | while | flops 61958 | bytes 67106 | solution.py:73
  307.0 0.8 fusion.75
  308.5 0.8 fusion.75
  310.0 0.8 fusion.75
  311.5 0.8 fusion.75
  313.0 0.8 fusion.75
  315.9 0.8 fusion.75
  317.4 0.8 fusion.75
  318.9 0.8 fusion.75
  320.4 0.8 fusion.75
  321.9 0.8 fusion.75
  323.4 0.8 fusion.75
  324.8 0.8 fusion.75
  326.3 0.8 fusion.75
  327.8 0.8 fusion.75
  329.3 0.8 fusion.75
  330.8 0.8 fusion.75
  332.3 0.8 fusion.75
  335.2 0.8 fusion.75
  336.7 0.8 fusion.75
  338.2 0.8 fusion.75
  339.7 0.8 fusion.75
  341.2 0.8 fusion.75
  344.1 0.8 fusion.75
  345.6 0.8 fusion.75
  347.1 0.8 fusion.75
  348.6 0.8 fusion.75
  350.1 0.8 fusion.75
  351.6 0.8 fusion.75
  353.1 0.8 fusion.75
  354.5 0.8 fusion.75
  356.0 0.8 fusion.75
  357.5 0.8 fusion.75
  359.0 0.8 fusion.75
  360.5 0.8 fusion.75
  363.5 0.8 fusion.75
  364.9 0.8 fusion.75
  366.4 0.8 fusion.75
  367.9 0.8 fusion.75
  369.4 0.8 fusion.75
  372.4 0.8 fusion.75
  373.9 0.8 fusion.75
  375.3 0.8 fusion.75
  376.8 0.8 fusion.75
  400.0 1.6 fusion.16
  401.6 1.2 copy.88
  (572 shorter events, 124.9 us)
Async XLA Ops:
  7.2 4.8 %copy-start = (f32[64,4,8,128]{3,2,1,0:T(8,128)S(1)}, f32[64,4,8,128]{3,2,1,0:T(8,128)}, u32[]{:S(2)}) copy-start(f32[64,4,8,128]{3,2,1,0:T(8,128)} %param.6) | copy-start | bytes 3145732
  7.2 5.0 %copy-start.1 = (f32[4,8,128]{2,1,0:T(8,128)S(1)}, f32[4,8,128]{2,1,0:T(8,128)}, u32[]{:S(2)}) copy-start(f32[4,8,128]{2,1,0:T(8,128)} %param.7) | copy-start | bytes 49156
  7.2 192.3 %all-gather.3.cloned.1.call-start = ((), (), s32[]{:S(2)}) async-start(), calls=%async_computation | async-start | bytes 8421376 | tf_op jit(solution)/shard_map/all_gather | solution.py:87
  8.6 9.6 %collective-permute-start = (f32[64,2,8,128]{3,2,1,0:T(8,128)S(1)}, f32[64,2,8,128]{3,2,1,0:T(8,128)S(1)}, u32[]{:S(2)}, u32[]{:S(2)}) collective-permute-start(f32[64,2,8,128]{3,2,1,0:T(8,128)S(1)} %get-tuple-element.276), channel_id=1, source_target_pairs={{8,0},{16,8},{24,16},{32,24},{40,32},{48,40},{56,48},{64,56},{72,6... | collective-permute-start | bytes 1572872 | tf_op jit(solution)/shard_map/ppermute | solution.py:16
  11.9 6.6 %collective-permute-start.1 = (f32[64,2,8,128]{3,2,1,0:T(8,128)S(1)}, f32[64,2,8,128]{3,2,1,0:T(8,128)S(1)}, u32[]{:S(2)}, u32[]{:S(2)}) collective-permute-start(f32[64,2,8,128]{3,2,1,0:T(8,128)S(1)} %get-tuple-element.275), channel_id=1, source_target_pairs={{0,8},{8,16},{16,24},{24,32},{32,40},{40,48},{48,56},{56,64},{64,7... | collective-permute-start | bytes 1572872 | tf_op jit(solution)/shard_map/ppermute | solution.py:14
  19.1 11.8 %collective-permute-start.2 = (f32[64,8,2,128]{3,1,2,0:T(8,128)S(1)}, f32[64,8,2,128]{3,1,2,0:T(8,128)S(1)}, u32[]{:S(2)}, u32[]{:S(2)}) collective-permute-start(f32[64,8,2,128]{3,1,2,0:T(8,128)S(1)} %get-tuple-element.263), channel_id=1, source_target_pairs={{1,0},{2,1},{3,2},{4,3},{5,4},{6,5},{7,6},{0,7},{9,8},{10,9},{11,1... | collective-permute-start | bytes 1572872 | tf_op jit(solution)/shard_map/ppermute | solution.py:16
  24.8 9.2 %collective-permute-start.3 = (f32[64,8,2,128]{3,1,2,0:T(8,128)S(1)}, f32[64,8,2,128]{3,1,2,0:T(8,128)S(1)}, u32[]{:S(2)}, u32[]{:S(2)}) collective-permute-start(f32[64,8,2,128]{3,1,2,0:T(8,128)S(1)} %get-tuple-element.264), channel_id=1, source_target_pairs={{0,1},{1,2},{2,3},{3,4},{4,5},{5,6},{6,7},{7,0},{8,9},{9,10},{10,1... | collective-permute-start | bytes 1572872 | tf_op jit(solution)/shard_map/ppermute | solution.py:14
  41.9 14.7 %collective-permute-start.4 = (f32[64,2,8,128]{3,2,1,0:T(8,128)S(1)}, f32[64,2,8,128]{3,2,1,0:T(8,128)S(1)}, u32[]{:S(2)}, u32[]{:S(2)}) collective-permute-start(f32[64,2,8,128]{3,2,1,0:T(8,128)S(1)} %copy.73), channel_id=1, source_target_pairs={{8,0},{16,8},{24,16},{32,24},{40,32},{48,40},{56,48},{64,56},{72,6... | collective-permute-start | bytes 1572872 | tf_op jit(solution)/shard_map/ppermute | solution.py:16
  51.7 6.4 %collective-permute-start.5 = (f32[64,2,8,128]{3,2,1,0:T(8,128)S(1)}, f32[64,2,8,128]{3,2,1,0:T(8,128)S(1)}, u32[]{:S(2)}, u32[]{:S(2)}) collective-permute-start(f32[64,2,8,128]{3,2,1,0:T(8,128)S(1)} %copy.75), channel_id=1, source_target_pairs={{0,8},{8,16},{16,24},{24,32},{32,40},{40,48},{48,56},{56,64},{64,7... | collective-permute-start | bytes 1572872 | tf_op jit(solution)/shard_map/ppermute | solution.py:14
  58.7 8.1 %collective-permute-start.6 = (f32[64,8,2,128]{3,1,2,0:T(8,128)S(1)}, f32[64,8,2,128]{3,1,2,0:T(8,128)S(1)}, u32[]{:S(2)}, u32[]{:S(2)}) collective-permute-start(f32[64,8,2,128]{3,1,2,0:T(8,128)S(1)} %get-tuple-element.261), channel_id=1, source_target_pairs={{1,0},{2,1},{3,2},{4,3},{5,4},{6,5},{7,6},{0,7},{9,8},{10,9},{11,1... | collective-permute-start | bytes 1572872 | tf_op jit(solution)/shard_map/ppermute | solution.py:16
  58.8 9.3 %collective-permute-start.7 = (f32[64,8,2,128]{3,1,2,0:T(8,128)S(1)}, f32[64,8,2,128]{3,1,2,0:T(8,128)S(1)}, u32[]{:S(2)}, u32[]{:S(2)}) collective-permute-start(f32[64,8,2,128]{3,1,2,0:T(8,128)S(1)} %get-tuple-element.262), channel_id=1, source_target_pairs={{0,1},{1,2},{2,3},{3,4},{4,5},{5,6},{6,7},{7,0},{8,9},{9,10},{10,1... | collective-permute-start | bytes 1572872 | tf_op jit(solution)/shard_map/ppermute | solution.py:14
  400.0 2.8 copy-start.2
Sparse Core Ops, SparseCore 0:
  78.4 120.9 all-gather.2
